TPU v7x, 512 devices: a whole 4x4x16 slice. The times are simulated.
512 devices in a mesh: strip: 512 (over z, y, x, core).
Axes of the slice: x: 4, y: 4, z: 16, core: 2. Of those that a mesh axis runs over, the one named last changes fastest.
Arguments:
- velocity: float32 [2, 128, 2048, 768], P(None, None, 'strip'), may hold values from -100 to 100
Outputs:
- spatial_modes: float32 [128, 2048, 768], P(None, 'strip')
- triangle: float32 [128, 128], replicated
All inputs are finite; a program needn't handle non-finite values.
Results may differ from a plain program's by a relative error of at most 0.000094.
Values sent between devices are 32-bit elements; how exact they have to be, the bound alone decides.
No kernel may reach another device: no remote copies, remote signals or barrier semaphores. Data moves between devices by JAX's collectives and lax.ppermute only.
A program may use at most 128 MiB of HBM per device.

v0:
```python
import jax
import jax.numpy as jnp
from jax import lax
from jax.sharding import PartitionSpec as P


def extended(array, sides, width):
    for axis, dim in sides:
        size, length = (lax.axis_size(axis), array.shape[dim])
        up = [(i, (i + 1) % size) for i in range(size)]
        down = [(j, i) for i, j in up]
        last = lax.slice_in_dim(array, length - width, length, axis=dim)
        initial = lax.slice_in_dim(array, 0, width, axis=dim)
        before = lax.ppermute(last, axis, up)
        after = lax.ppermute(initial, axis, down)
        array = jnp.concatenate([before, array, after], axis=dim)
    return array


def along_second(field):
    return (
        8.0 * (jnp.roll(field, -1, 2) - jnp.roll(field, 1, 2))
        - (jnp.roll(field, -2, 2) - jnp.roll(field, 2, 2))
    ) / 12.0


def stencil_rows(padded, row_count):
    return 8.0 * (padded[:, 3 : row_count + 3] - padded[:, 1 : row_count + 1]) - (
        padded[:, 4 : row_count + 4] - padded[:, 0:row_count]
    )


def local(velocity):
    snap_count = velocity.shape[1]
    row_count = velocity.shape[2]
    col_count = velocity.shape[3]
    total_cells = row_count * lax.axis_size("strip") * col_count
    comp_u = velocity[0]
    comp_v = velocity[1]
    padded = extended(comp_v, (("strip", 1),), 2)
    v_first = stencil_rows(padded, row_count) / 12.0
    vorticity = v_first - along_second(comp_u)
    flattened = vorticity.reshape(snap_count, row_count * col_count)
    local_gram = (
        jnp.dot(
            flattened,
            flattened.T,
            precision=lax.Precision.HIGHEST,
            preferred_element_type=jnp.float32,
        )
        / total_cells
    )
    gram = lax.psum(local_gram, "strip")
    lower = jnp.linalg.cholesky(gram)
    identity = jnp.eye(snap_count, dtype=jnp.float32)
    inverse_lower = lax.linalg.triangular_solve(lower, identity, left_side=True, lower=True)
    spatial_modes = jnp.dot(
        inverse_lower,
        flattened,
        precision=lax.Precision.HIGHEST,
        preferred_element_type=jnp.float32,
    )
    return (spatial_modes.reshape(snap_count, row_count, col_count), lower.T)


def solution(mesh):
    return jax.shard_map(
        local,
        mesh=mesh,
        in_specs=(P(None, None, "strip", None),),
        out_specs=(P(None, "strip", None), P()),
        check_vma=False,
    )
```

profile of v0, /device:TPU:1, one launch (start us, length us, event | category | flops | bytes accessed | tf_op | source)
XLA Modules:
  0.0 519.4 jit_solution(6703230414431210953)
XLA Ops:
  7.2 2.4 slice_bitcast_fusion
  9.6 0.6 fusion.26
  10.2 8.8 %collective-permute-start = (f32[128,2,768]{2,1,0:T(2,128)S(1)}, f32[128,2,768]{2,1,0:T(2,128)S(1)}, u32[]{:S(2)}, u32[]{:S(2)}) collective-permute-start(f32[128,2,768]{2,1,0:T(2,128)S(1)} %get-tuple-element.14), channel_id=1, source_target_pairs={{1,0},{2,1},{3,2},{4,3},{5,4},{6,5},{7,6},{8,7},{9,8},{10,9},{11,1... | collective-permute-start | bytes 2359304 | tf_op jit(solution)/shard_map/ppermute | solution.py:15
  19.0 1.9 collective-permute-start.1
  21.2 0.2 fusion.22
  21.4 0.9 fusion.25
  22.3 0.9 fusion.23
  23.2 1.2 collective-permute-done
  24.4 6.5 %collective-permute-done.1 = f32[128,2,768]{2,1,0:T(2,128)S(1)} collective-permute-done((f32[128,2,768]{2,1,0:T(2,128)S(1)}, f32[128,2,768]{2,1,0:T(2,128)S(1)}, u32[]{:S(2)}, u32[]{:S(2)}) %collective-permute-start.1) | collective-permute-done | bytes 786464 | tf_op jit(solution)/shard_map/ppermute | solution.py:14
  30.9 5.1 fusion.5
  36.0 2.3 fusion.16
  38.3 0.3 copy.12
  38.6 0.5 copy.7
  39.1 444.1 %all-reduce.2.cloned.1.call-done = f32[128,128]{0,1:T(8,128)} async-done(((f32[128,128]{0,1:T(8,128)}), f32[128,128]{0,1:T(8,128)}) %all-reduce.2.cloned.1.call-update) | async-done | bytes 65552 | tf_op jit(solution)/shard_map/psum | solution.py:53
  483.2 0.9 copy.6
  484.1 0.9 fusion.20
  485.0 11.7 %cholesky.17 = f32[128,128]{1,0:T(8,128)S(1)} custom-call(f32[128,128]{1,0:T(8,128)S(1)} %fusion.20), custom_call_target="Cholesky" | custom-call | tf_op jit(solution)/shard_map/jit(cholesky)/cholesky | solution.py:54
  496.8 0.6 compare_reduce_fusion
  497.4 0.7 fusion.21
  498.1 9.8 %custom-call.6 = f32[1,128,128]{1,2,0:T(8,128)S(1)} custom-call(f32[1,128,128]{2,1,0:T(8,128)S(1)} %get-tuple-element.17), custom_call_target="InvertDiagBlocksLowerTriangular" | custom-call | tf_op jit(solution)/shard_map/triangular_solve | solution.py:56
  507.9 0.2 convolution_bitcast_fusion
  508.1 1.5 fusion.27
  509.6 2.2 copy.8
  511.8 0.7 copy.9
  (4 shorter events, 0.3 us)
Async XLA Ops:
  7.2 476.1 %all-reduce.2.cloned.1.call-start = ((), (), s32[]{:S(2)}) async-start(), calls=%async_computation | async-start | bytes 131072 | tf_op jit(solution)/shard_map/psum | solution.py:53
  10.2 14.2 %collective-permute-start = (f32[128,2,768]{2,1,0:T(2,128)S(1)}, f32[128,2,768]{2,1,0:T(2,128)S(1)}, u32[]{:S(2)}, u32[]{:S(2)}) collective-permute-start(f32[128,2,768]{2,1,0:T(2,128)S(1)} %get-tuple-element.14), channel_id=1, source_target_pairs={{1,0},{2,1},{3,2},{4,3},{5,4},{6,5},{7,6},{8,7},{9,8},{10,9},{11,1... | collective-permute-start | bytes 2359304 | tf_op jit(solution)/shard_map/ppermute | solution.py:15
  19.0 11.9 %collective-permute-start.1 = (f32[128,2,768]{2,1,0:T(2,128)S(1)}, f32[128,2,768]{2,1,0:T(2,128)S(1)}, u32[]{:S(2)}, u32[]{:S(2)}) collective-permute-start(f32[128,2,768]{2,1,0:T(2,128)S(1)} %get-tuple-element.15), channel_id=1, source_target_pairs={{0,1},{1,2},{2,3},{3,4},{4,5},{5,6},{6,7},{7,8},{8,9},{9,10},{10,1... | collective-permute-start | bytes 2359304 | tf_op jit(solution)/shard_map/ppermute | solution.py:14
Sparse Core Ops, SparseCore 0:
  38.5 444.7 all-reduce.1
where the time goes:
time: 520 us; the launch traced here: 519 us
  waiting for transfers between devices  452 us (87%)
  other arithmetic  28.8 us (6%)
  between operations  14.1 us (3%)
  starting transfers between devices  10.7 us (2%)
  local copies, waits for them, and re-layouts  9.79 us (2%)
    psum x1, waiting for transfers between devices, local(): gram = lax.psum(local_gram, 'strip')  444 us
    another operation x3, other arithmetic, local(): lower = jnp.linalg.cholesky(gram)  12.4 us
  transfers between devices with their start and end apart: 3, of which 3 were waited for; matrix products, arithmetic and copies ran while one was open for 1% of the time, Pallas kernels for 0%

commit v1 on v0

--- a/solution.py
+++ b/solution.py
@@ -50,7 +50,7 @@
         )
         / total_cells
     )
-    gram = lax.psum(local_gram, "strip")
+    gram = jnp.sum(jax.lax.all_gather(local_gram, "strip"), axis=0)
     lower = jnp.linalg.cholesky(gram)
     identity = jnp.eye(snap_count, dtype=jnp.float32)
     inverse_lower = lax.linalg.triangular_solve(lower, identity, left_side=True, lower=True)

time: 520 us -> 329 us (0.63)
  waiting for transfers between devices: 452 us -> 250 us
  other arithmetic: 28.8 us -> 41 us
    psum x1 -> x0, waiting for transfers between devices: 444 us -> none  [local(): gram = lax.psum(local_gram, 'strip')]
    all_gather x0 -> x1, waiting for transfers between devices: none -> 242 us  [local(): gram = jnp.sum(jax.lax.all_gather(local_gram, 'strip'), axis=0)]
    reduce_sum x0 -> x1, other arithmetic: none -> 13.3 us  [local(): gram = jnp.sum(jax.lax.all_gather(local_gram, 'strip'), axis=0)]
where the time goes in v1:
time: 329 us
  waiting for transfers between devices  250 us (76%)
  other arithmetic  41 us (12%)
  between operations  14.1 us (4%)
  starting transfers between devices  10.7 us (3%)
  local copies, waits for them, and re-layouts  8.95 us (3%)
  matrix products  4.07 us (1%)
    all_gather x1, waiting for transfers between devices, local(): gram = jnp.sum(jax.lax.all_gather(local_gram, 'strip'), axis=0)  242 us
    reduce_sum x1, other arithmetic, local(): gram = jnp.sum(jax.lax.all_gather(local_gram, 'strip'), axis=0)  13.3 us
    another operation x3, other arithmetic, local(): lower = jnp.linalg.cholesky(gram)  12.4 us
    another operation x1, other arithmetic, local(): lax.linalg.triangular_solve(lower, identity, left_side=True, lower=True)  9.81 us
    ppermute x1, starting transfers between devices, extended(): after = lax.ppermute(initial, axis, down)  8.79 us
  transfers between devices with their start and end apart: 3, of which 3 were waited for; matrix products, arithmetic and copies ran while one was open for 1% of the time, Pallas kernels for 0%

profile of v1, /device:TPU:1, one launch (start us, length us, event | category | flops | bytes accessed | tf_op | source)
XLA Modules:
  0.0 328.6 jit_solution(2331024837784504634)
XLA Ops:
  7.2 2.4 slice_bitcast_fusion
  9.6 0.6 fusion.26
  10.2 8.8 %collective-permute-start = (f32[128,2,768]{2,1,0:T(2,128)S(1)}, f32[128,2,768]{2,1,0:T(2,128)S(1)}, u32[]{:S(2)}, u32[]{:S(2)}) collective-permute-start(f32[128,2,768]{2,1,0:T(2,128)S(1)} %get-tuple-element.16), channel_id=1, source_target_pairs={{1,0},{2,1},{3,2},{4,3},{5,4},{6,5},{7,6},{8,7},{9,8},{10,9},{11,1... | collective-permute-start | bytes 2359304 | tf_op jit(solution)/shard_map/ppermute | solution.py:15
  19.0 1.9 collective-permute-start.1
  21.0 0.2 fusion.24
  21.2 0.2 fusion.22
  21.4 0.9 fusion.25
  22.3 0.9 fusion.23
  23.2 1.2 collective-permute-done
  24.4 6.5 %collective-permute-done.1 = f32[128,2,768]{2,1,0:T(2,128)S(1)} collective-permute-done((f32[128,2,768]{2,1,0:T(2,128)S(1)}, f32[128,2,768]{2,1,0:T(2,128)S(1)}, u32[]{:S(2)}, u32[]{:S(2)}) %collective-permute-start.1) | collective-permute-done | bytes 786464 | tf_op jit(solution)/shard_map/ppermute | solution.py:14
  30.9 4.9 %fusion.5 = f32[128,4,768]{2,1,0:T(4,128)S(1)} fusion(f32[128,2,768]{2,1,0:T(2,128)S(1)} %collective-permute-done.1, f32[128,4,768]{2,1,0:T(4,128)S(1)} %get-tuple-element.7, f32[128,2,768]{2,1,0:T(2,128)S(1)} %collective-permute-done, f32[128,4,1]{2,1,0:T(4,128)S(1)} %get-tuple-element.13, f32[128,4,767]{2,1,0:T(4,128)S(1)} %get-tuple-element.15, ...), kind=kLoop, calls=%fused_computation.9 | loop fusion | flops 7471104 | bytes 11010048 | tf_op jit(solution)/shard_map/sub | solution.py:42
  35.8 2.3 fusion.16
  38.2 0.3 copy.15
  38.5 0.5 copy.12
  38.9 241.9 %all-gather.3.cloned.1.call-done = f32[65536,128]{1,0:T(8,128)} async-done(((f32[128,128]{1,0:T(8,128)}), f32[65536,128]{1,0:T(8,128)}) %all-gather.3.cloned.1.call-update) | async-done | bytes 33554448 | tf_op jit(solution)/shard_map/all_gather | solution.py:53
  280.8 13.3 %reduce_sum.9 = f32[128,128]{1,0:T(8,128)S(1)} reduce(f32[512,128,128]{2,1,0:T(8,128)} %bitcast.29, f32[]{:T(128)} %constant.47.clone.1), dimensions={0}, to_apply=%region_0.1 | reduce | flops 8372224 | bytes 33619972 | tf_op jit(solution)/shard_map/reduce_sum | solution.py:53
  294.2 11.7 %cholesky.17 = f32[128,128]{1,0:T(8,128)S(1)} custom-call(f32[128,128]{1,0:T(8,128)S(1)} %fusion.20), custom_call_target="Cholesky" | custom-call | tf_op jit(solution)/shard_map/jit(cholesky)/cholesky | solution.py:54
  306.0 0.6 compare_reduce_fusion
  306.6 0.7 fusion.21
  307.3 0.7 copy.14
  308.0 9.8 %custom-call.6 = f32[1,128,128]{1,2,0:T(8,128)S(1)} custom-call(f32[1,128,128]{2,1,0:T(8,128)S(1)} %get-tuple-element.19), custom_call_target="InvertDiagBlocksLowerTriangular" | custom-call | tf_op jit(solution)/shard_map/triangular_solve | solution.py:56
  317.8 0.2 convolution_bitcast_fusion
  318.1 1.5 fusion.27
  319.6 2.2 copy.13
  (5 shorter events, 0.2 us)
Async XLA Ops:
  7.2 273.7 %all-gather.3.cloned.1.call-start = ((), (), s32[]{:S(2)}) async-start(), calls=%async_computation | async-start | bytes 33619968 | tf_op jit(solution)/shard_map/all_gather | solution.py:53
  10.2 14.2 %collective-permute-start = (f32[128,2,768]{2,1,0:T(2,128)S(1)}, f32[128,2,768]{2,1,0:T(2,128)S(1)}, u32[]{:S(2)}, u32[]{:S(2)}) collective-permute-start(f32[128,2,768]{2,1,0:T(2,128)S(1)} %get-tuple-element.16), channel_id=1, source_target_pairs={{1,0},{2,1},{3,2},{4,3},{5,4},{6,5},{7,6},{8,7},{9,8},{10,9},{11,1... | collective-permute-start | bytes 2359304 | tf_op jit(solution)/shard_map/ppermute | solution.py:15
  19.0 11.9 %collective-permute-start.1 = (f32[128,2,768]{2,1,0:T(2,128)S(1)}, f32[128,2,768]{2,1,0:T(2,128)S(1)}, u32[]{:S(2)}, u32[]{:S(2)}) collective-permute-start(f32[128,2,768]{2,1,0:T(2,128)S(1)} %get-tuple-element.17), channel_id=1, source_target_pairs={{0,1},{1,2},{2,3},{3,4},{4,5},{5,6},{6,7},{7,8},{8,9},{9,10},{10,1... | collective-permute-start | bytes 2359304 | tf_op jit(solution)/shard_map/ppermute | solution.py:14
Sparse Core Ops, SparseCore 0:
  38.3 242.4 all-gather.2
